TPU v7x, 512 devices: a whole 4x8x8 slice. The times are simulated.
512 devices in a mesh: seq: 16 (over z, core), expert: 32 (over x, y).
Axes of the slice: x: 4, y: 8, z: 8, core: 2. Of those that a mesh axis runs over, the one named last changes fastest.
Arguments:
- hidden: bfloat16 [32, 1024, 2048], P('expert', 'seq'), may hold values from -6 to 6
- queries: bfloat16 [32, 1024, 4608], P('expert', 'seq'), may hold values from -5 to 5
- suffix_latent: bfloat16 [32, 1024, 576], P('expert', 'seq'), may hold values from -6 to 6
- prefix_latent: bfloat16 [2, 1024, 576], P(None, 'seq'), may hold values from -6 to 6
- lengths: int32 [32, 4], P('expert'), may hold values from 1 to 512, 1024 in all within a row
- prefix_of: int32 [32, 4], P('expert'), may hold values from 0 to 1
- value_up: bfloat16 [8, 512, 128], replicated, may hold values from -1 to 1
- out_proj: bfloat16 [1024, 2048], P(None, 'expert'), may hold values from -0.1875 to 0.1875
- norm_gain: float32 [2048], replicated, may hold values from 0.5 to 1.5
- router: bfloat16 [2048, 32], replicated, may hold values from -0.0625 to 0.0625
- routes: int32 [32, 1024, 6], P('expert', 'seq'), may hold values from 0 to 31, all different within a row; in each aligned block of 64 rows (0 to 63, 64 to 127, ..., all dimensions but the last counted through in order) at most 16 rows name the same one
- expert_in: bfloat16 [32, 2048, 1408], P('expert', 'seq'), may hold values from -0.125 to 0.125
- expert_out: bfloat16 [32, 2048, 704], P('expert', 'seq'), may hold values from -1.25 to 1.25
Outputs:
- layer_out: bfloat16 [32, 1024, 2048], P('expert', 'seq')
Inputs may be any that keep to these rules, and one draw needn't show every extreme that they name: `routes`: among the rows of one device (aligned blocks of 64 tokens) no expert is named more than 16 times, a bound that some block reaches; a token's 6 experts differ. `lengths`: each row sums to 1024; its longest request has exactly 512 tokens.
All inputs are finite; a program needn't handle non-finite values.
Results may differ from a plain program's by a relative error of at most 0.013.
Values may be sent and summed in bfloat16 or wider, within the bound.
No kernel may reach another device: no remote copies, remote signals or barrier semaphores. Data moves between devices by JAX's collectives and lax.ppermute only.
A program may use at most 128 MiB of HBM per device.

v0:
```python
import jax
import jax.numpy as jnp
from jax import lax
from jax.sharding import PartitionSpec as P

qk_scale = 192.0 ** (-0.5)
big_negative = -1e30


def request_of(positions, request_ends):
    return jnp.sum((positions[:, None] >= request_ends[None, :]).astype(jnp.int32), axis=1)


def merge_scores(running, scores, allowed, values):
    running_max, running_sum, running_acc = running
    new_max = jnp.maximum(running_max, jnp.max(jnp.where(allowed, scores, big_negative), axis=2))
    weights = jnp.where(allowed, jnp.exp(scores - new_max[:, :, None]), 0.0)
    new_sum = jnp.sum(weights, axis=2)
    new_acc = jnp.einsum(
        "thn,nl->thl", weights.astype(jnp.bfloat16), values, preferred_element_type=jnp.float32
    )
    return (new_max, new_sum, new_acc)


def local(
    hidden,
    queries,
    suffix_latent,
    prefix_latent,
    lengths,
    prefix_of,
    value_up,
    out_proj,
    norm_gain,
    router,
    routes,
    expert_in,
    expert_out,
):
    local_tokens = hidden.shape[1]
    model_width = hidden.shape[2]
    key_width = suffix_latent.shape[2]
    head_count = value_up.shape[0]
    latent_width = value_up.shape[1]
    expert_count = router.shape[1]
    top_count = routes.shape[2]
    capacity = 4 * local_tokens * top_count // (3 * expert_count)
    request_count = lengths.shape[1]
    request_ends = jnp.cumsum(lengths[0])
    my_positions = lax.axis_index("seq") * local_tokens + jnp.arange(local_tokens, dtype=jnp.int32)
    my_requests = request_of(my_positions, request_ends)
    request_ids = jnp.arange(request_count, dtype=jnp.int32)
    chosen = jnp.sum(
        jnp.where(my_requests[:, None] == request_ids[None, :], prefix_of[0][None, :], 0), axis=1
    )
    prefix_pick = chosen[:, None] == jnp.arange(2, dtype=jnp.int32)[None, :]
    single_prefix = jnp.all(chosen == chosen[0])
    my_prefix = chosen[0]
    query_rows = queries[0].reshape(local_tokens, head_count, key_width)
    start_state = (
        jnp.full((local_tokens, head_count), big_negative, jnp.float32),
        jnp.zeros((local_tokens, head_count), jnp.float32),
        jnp.zeros((local_tokens, head_count, latent_width), jnp.float32),
    )
    suffix_piece = lax.all_gather(suffix_latent, "seq", axis=1, tiled=True)
    prefix_piece = lax.all_gather(prefix_latent, "seq", axis=1, tiled=True)
    piece_rows = suffix_piece.shape[1]
    suffix_keys = suffix_piece[0]
    key_positions = jnp.arange(piece_rows, dtype=jnp.int32)
    key_requests = request_of(key_positions, request_ends)
    suffix_allowed = (key_requests[None, :] == my_requests[:, None]) & (
        key_positions[None, :] <= my_positions[:, None]
    )
    suffix_scores = (
        jnp.einsum("thk,nk->thn", query_rows, suffix_keys, preferred_element_type=jnp.float32)
        * qk_scale
    )

    def one_prefix(running_state):
        chosen_keys = lax.dynamic_index_in_dim(prefix_piece, my_prefix, 0, keepdims=False)
        prefix_scores = (
            jnp.einsum("thk,nk->thn", query_rows, chosen_keys, preferred_element_type=jnp.float32)
            * qk_scale
        )
        scores = jnp.concatenate([suffix_scores, prefix_scores], axis=2)
        every_key = jnp.ones((local_tokens, piece_rows), dtype=bool)
        allowed = jnp.concatenate([suffix_allowed, every_key], axis=1)[:, None, :]
        values = jnp.concatenate(
            [suffix_keys[:, :latent_width], chosen_keys[:, :latent_width]], axis=0
        )
        return merge_scores(running_state, scores, allowed, values)

    def two_prefixes(running_state):
        prefix_scores = (
            jnp.einsum(
                "thk,pnk->thpn", query_rows, prefix_piece, preferred_element_type=jnp.float32
            )
            * qk_scale
        )
        scores = jnp.concatenate(
            [suffix_scores, prefix_scores.reshape(local_tokens, head_count, 2 * piece_rows)], axis=2
        )
        prefix_allowed = jnp.broadcast_to(
            prefix_pick[:, :, None], (local_tokens, 2, piece_rows)
        ).reshape(local_tokens, 2 * piece_rows)
        allowed = jnp.concatenate([suffix_allowed, prefix_allowed], axis=1)[:, None, :]
        values = jnp.concatenate(
            [
                suffix_keys[:, :latent_width],
                prefix_piece[:, :, :latent_width].reshape(2 * piece_rows, latent_width),
            ],
            axis=0,
        )
        return merge_scores(running_state, scores, allowed, values)

    final_max, final_sum, final_acc = lax.cond(single_prefix, one_prefix, two_prefixes, start_state)
    latent_out = (final_acc / final_sum[:, :, None]).astype(jnp.bfloat16)
    value_out = jnp.einsum(
        "thl,hlv->thv", latent_out, value_up, preferred_element_type=jnp.float32
    ).astype(jnp.bfloat16)
    value_out = value_out.reshape(local_tokens, head_count * value_up.shape[2])
    projected = jnp.dot(
        value_out,
        lax.all_gather(out_proj, "expert", axis=1, tiled=True),
        preferred_element_type=jnp.float32,
    )
    residual = hidden[0].astype(jnp.float32) + projected
    normed = (
        residual
        * lax.rsqrt(jnp.mean(residual * residual, axis=1, keepdims=True) + 1e-06)
        * norm_gain
    ).astype(jnp.bfloat16)
    logits = jnp.dot(normed, router, preferred_element_type=jnp.float32)
    expert_probs = jax.nn.softmax(logits, axis=1)
    expert_ids = jnp.arange(expert_count, dtype=jnp.int32)
    my_routes = routes[0]
    matches = my_routes[:, :, None] == expert_ids[None, None, :]
    gate_values = jnp.sum(jnp.where(matches, expert_probs[:, None, :], 0.0), axis=2)
    flat_hits = matches.reshape(local_tokens * top_count, expert_count).astype(jnp.int32)
    earlier = jnp.cumsum(flat_hits, axis=0) - flat_hits
    slot_index = jnp.sum(earlier * flat_hits, axis=1).reshape(local_tokens, top_count)
    cell_index = my_routes * capacity + slot_index
    cell_ids = jnp.arange(expert_count * capacity, dtype=jnp.int32)
    placing = jnp.sum(
        (cell_ids[:, None, None] == cell_index[None, :, :]).astype(jnp.int32), axis=2
    ).astype(jnp.bfloat16)
    outgoing = jnp.dot(placing, normed, preferred_element_type=jnp.float32).astype(jnp.bfloat16)
    outgoing = outgoing.reshape(expert_count, capacity, model_width)
    incoming = lax.all_to_all(outgoing, "expert", split_axis=0, concat_axis=0, tiled=True)
    full_in, full_out = (
        lax.all_gather(expert_in, "seq", axis=1, tiled=True),
        lax.all_gather(expert_out, "seq", axis=1, tiled=True),
    )
    all_rows = incoming.reshape(-1, model_width)
    gate_up = jnp.dot(all_rows, full_in[0], preferred_element_type=jnp.float32)
    hidden_units = gate_up.shape[1] // 2
    active = (jax.nn.silu(gate_up[:, :hidden_units]) * gate_up[:, hidden_units:]).astype(
        jnp.bfloat16
    )
    produced = lax.dot_general(
        active, full_out[0], (((1,), (1,)), ((), ())), preferred_element_type=jnp.float32
    ).astype(jnp.bfloat16)
    returned = lax.all_to_all(
        produced.reshape(-1, capacity, model_width),
        "expert",
        split_axis=0,
        concat_axis=0,
        tiled=True,
    )
    returned_rows = returned.reshape(-1, model_width)
    picked = returned_rows[cell_index]
    routed_sum = jnp.sum(gate_values[:, :, None] * picked.astype(jnp.float32), axis=1)
    layer_out = (residual + routed_sum).astype(jnp.bfloat16)
    return layer_out[None]


def solution(mesh):
    in_specs = (
        P("expert", "seq", None),
        P("expert", "seq", None),
        P("expert", "seq", None),
        P(None, "seq", None),
        P("expert", None),
        P("expert", None),
        P(),
        P(None, "expert"),
        P(),
        P(),
        P("expert", "seq", None),
        P("expert", "seq", None),
        P("expert", "seq", None),
    )
    out_specs = P("expert", "seq", None)
    return jax.shard_map(local, mesh=mesh, in_specs=in_specs, out_specs=out_specs, check_vma=False)
```

profile of v0, /device:TPU:16, one launch (start us, length us, event | category | flops | bytes accessed | tf_op | source)
XLA Modules:
  0.0 368.0 jit_solution(16596417180253832410)
XLA Ops:
  6.5 0.7 all-gather.8.cloned.1.call-update
  7.3 0.0 all-gather.6.cloned.1.call-start
  7.3 1.8 copy.86
  9.1 0.0 all-gather.10.cloned.1.call-start
  9.1 0.7 all-gather.10.cloned.1.call-update
  9.9 0.5 all-gather.12.cloned.1.call-update
  10.4 0.5 all-gather.14.cloned.1.call-update
  11.0 0.8 copy.97
  11.8 0.1 eq.114
  11.9 0.1 eq.110
  12.1 0.8 reduce-window.18
  12.9 0.1 convert_reduce_fusion.1
  13.0 0.1 convert_reduce_fusion.2
  13.1 0.1 fusion.38
  13.2 0.7 select_reduce_fusion.3
  13.9 2.4 reshape_squeeze.3
  16.4 0.7 compare_reduce_fusion
  17.7 0.9 reduce-window.19
  18.6 0.2 slice_reduce_fusion
  18.9 0.1 fusion.44
  19.0 0.1 reshape.139
  19.1 0.1 copy.101
  19.2 0.8 convert_reduce_fusion
  20.0 36.3 %all-gather.8.cloned.1.call-done = bf16[1,1024,576]{2,1,0:T(8,128)(2,1)} async-done(((bf16[1,64,576]{2,1,0:T(8,128)(2,1)}), bf16[1,1024,576]{2,1,0:T(8,128)(2,1)}) %all-gather.8.cloned.1.call-update) | async-done | bytes 1179664 | tf_op jit(solution)/shard_map/all_gather | solution.py:65
  56.3 2.4 copy.87
  58.7 2.5 convolution_multiply_fusion
  61.3 39.0 %all-gather.6.cloned.1.call-done = bf16[2,1024,576]{2,0,1:T(2,128)(2,1)} async-done(((bf16[2,64,576]{2,0,1:T(2,128)(2,1)}), bf16[2,1024,576]{2,0,1:T(2,128)(2,1)}) %all-gather.6.cloned.1.call-update) | async-done | bytes 2359312 | tf_op jit(solution)/shard_map/all_gather | solution.py:66
  100.3 31.3 %conditional.1 = (f32[64,8,512]{2,1,0:T(8,128)}, f32[64,8]{1,0:T(8,128)S(1)}) conditional(s32[]{:T(128)} %convert_element_type.64, (s32[64]{0:T(128)S(1)}, s32[64,2]{1,0:T(8,128)S(1)}, pred[64,1024]{1,0:T(8,128)(4,1)S(1)}, bf16[64,8,576]{2,1,0:T(8,128)(2,1)}, bf16[2,1024,576]{2,0,1:T(2,128)(2,1)}, /*index=5*/f32[64,8,1024]{2,1,0:T(8,128)S(1)}, ...), branch_computations={%region_5.8_spmd, %region_8.11_spmd} | conditional | flops 2843409920 | bytes 92157032 | solution.py:116
  100.3 7.4 %copy.88 = bf16[2,1024,576]{1,2,0:T(8,128)(2,1)} copy(bf16[2,1024,576]{2,0,1:T(2,128)(2,1)} %get-tuple-element.110) | data formatting | bytes 4718592 | tf_op jit(solution)/shard_map
  107.6 3.7 fusion.10
  111.3 0.1 broadcast_compare_fusion
  111.4 0.2 broadcast_in_dim.61
  111.6 0.1 copy.108
  111.7 1.2 select_reduce_fusion
  112.9 0.5 copy-done.1
  113.4 1.1 copy-done.4
  114.5 1.5 slice.36
  116.0 4.0 %copy.82 = bf16[2,1024,512]{2,1,0:T(8,128)(2,1)} copy(bf16[2,1024,512]{1,2,0:T(8,128)(2,1)} %slice.36) | data formatting | bytes 4194304 | tf_op jit(solution)/shard_map/cond/branch_0_fun/slice | solution.py:110
  120.0 2.4 copy.89
  122.4 1.3 slice.35
  123.7 5.9 %fusion.2 = f32[64,8,512]{2,1,0:T(8,128)} fusion(bf16[2048,512]{1,0:T(8,128)(2,1)} %bitcast.104, bf16[1024,512]{1,0:T(8,128)(2,1)S(1)} %slice.35, f32[64,8,2048]{2,1,0:T(8,128)} %bitcast.98, f32[64,8,1024]{2,1,0:T(8,128)S(1)} %get-tuple-element.36, f32[64,8]{1,0:T(8,128)S(1)} %broadcast_maximum_fusion, pred[64,3072]{1,0:T(8,128)(4,1)S(1)} %pad_add_fusion), kind=kOutput, calls=%fused_computation.7 | convolution fusion | flops 1623195648 | bytes 10684416 | tf_op jit(solution)/shard_map/cond/branch_0_fun/thn,nl->thl/dot_general | solution.py:19
  129.6 1.8 fusion.1
  131.5 1.4 divide_convert_fusion
  133.0 0.4 fusion.33
  133.4 54.2 %all-gather.10.cloned.1.call-done = bf16[1024,2048]{0,1:T(8,128)(2,1)} async-done(((bf16[1024,64]{0,1:T(8,128)(2,1)}), bf16[1024,2048]{0,1:T(8,128)(2,1)}) %all-gather.10.cloned.1.call-update) | async-done | bytes 4194320 | tf_op jit(solution)/shard_map/all_gather | solution.py:124
  187.6 3.7 %multiply_reduce_fusion.1 = (f32[64]{0:T(128)S(1)}, f32[64,2048]{1,0:T(8,128)S(1)}) fusion(bf16[1024,2048]{0,1:T(8,128)(2,1)} %all-gather.10.cloned.1.call-done, bf16[8,8,8,128]{3,2,1,0:T(8,128)(2,1)S(1)} %fusion.33, bf16[1,64,2048]{2,1,0:T(8,128)(2,1)S(1)} %copy-done.9), kind=kOutput, calls=%fused_computation.60 | convolution fusion | flops 268959680 | bytes 5112064 | tf_op jit(solution)/shard_map/dot_general | solution.py:122
  191.3 0.8 copy-done.5
  192.1 2.1 convolution_convert_fusion.1
  194.1 7.2 %all-to-all-start = ((bf16[32,16,2048]{2,1,0:T(8,128)(2,1)}), bf16[32,16,2048]{2,1,0:T(8,128)(2,1)S(1)}, u32[]{:S(2)}, u32[]{:S(2)}) async-start(bf16[32,16,2048]{2,1,0:T(8,128)(2,1)} %bitcast.20), calls=%async_computation | async-start | bytes 4194304 | tf_op jit(solution)/shard_map/all_to_all | solution.py:149
  201.3 34.9 %all-gather.12.cloned.1.call-done = bf16[1,2048,1408]{2,1,0:T(8,128)(2,1)} async-done(((bf16[1,128,1408]{2,1,0:T(8,128)(2,1)}), bf16[1,2048,1408]{2,1,0:T(8,128)(2,1)}) %all-gather.12.cloned.1.call-update) | async-done | bytes 5767184 | tf_op jit(solution)/shard_map/all_gather | solution.py:151
  236.2 11.3 %all-to-all-done = bf16[32,16,2048]{2,1,0:T(8,128)(2,1)S(1)} async-done(((bf16[32,16,2048]{2,1,0:T(8,128)(2,1)}), bf16[32,16,2048]{2,1,0:T(8,128)(2,1)S(1)}, u32[]{:S(2)}, u32[]{:S(2)}) %all-to-all-start) | async-done | bytes 2097184 | tf_op jit(solution)/shard_map/all_to_all | solution.py:149
  247.5 7.6 %fusion.28 = f32[512,1408]{1,0:T(8,128)} fusion(bf16[512,2048]{1,0:T(8,128)(2,1)S(1)} %bitcast.103, bf16[1,2048,1408]{2,1,0:T(8,128)(2,1)} %all-gather.12.cloned.1.call-done), kind=kOutput, calls=%fused_computation.40 | convolution fusion | flops 2952790016 | bytes 10747904 | tf_op jit(solution)/shard_map/dot_general | solution.py:155
  255.2 28.3 %all-gather.14.cloned.1.call-done = bf16[1,2048,704]{1,2,0:T(8,128)(2,1)} async-done(((bf16[1,128,704]{1,2,0:T(8,128)(2,1)}), bf16[1,2048,704]{1,2,0:T(8,128)(2,1)}) %all-gather.14.cloned.1.call-update) | async-done | bytes 2883600 | tf_op jit(solution)/shard_map/all_gather | solution.py:152
  283.5 6.0 %convolution_convert_fusion = bf16[512,2048]{1,0:T(8,128)(2,1)} fusion(bf16[1,2048,704]{1,2,0:T(8,128)(2,1)} %all-gather.14.cloned.1.call-done, f32[512,1408]{1,0:T(8,128)} %fusion.28), kind=kOutput, calls=%fused_computation.43 | convolution fusion | flops 1479606272 | bytes 8126464 | tf_op jit(solution)/shard_map/dot_general | solution.py:160
  289.5 10.0 %all-to-all-start.1 = ((bf16[32,16,2048]{2,1,0:T(8,128)(2,1)}), bf16[32,16,2048]{2,1,0:T(8,128)(2,1)S(1)}, u32[]{:S(2)}, u32[]{:S(2)}) async-start(bf16[32,16,2048]{2,1,0:T(8,128)(2,1)} %bitcast.102), calls=%async_computation.1 | async-start | bytes 4194304 | tf_op jit(solution)/shard_map/all_to_all | solution.py:163
  299.5 0.1 reshape.144
  299.6 0.1 reshape.148
  299.8 1.3 fusion.50
  301.2 0.1 copy.96
  301.3 48.6 %all-to-all-done.1 = bf16[32,16,2048]{2,1,0:T(8,128)(2,1)S(1)} async-done(((bf16[32,16,2048]{2,1,0:T(8,128)(2,1)}), bf16[32,16,2048]{2,1,0:T(8,128)(2,1)S(1)}, u32[]{:S(2)}, u32[]{:S(2)}) %all-to-all-start.1) | async-done | bytes 2097184 | tf_op jit(solution)/shard_map/all_to_all | solution.py:163
  349.9 3.1 gather_fusion
  353.0 3.9 %reshape.155 = f32[64,6,2048]{2,1,0:T(8,128)} reshape(bf16[384,2048]{1,0:T(8,128)(2,1)} %gather_fusion) | data formatting | bytes 4718592 | tf_op jit(solution)/shard_map/convert_element_type | solution.py:172
  356.9 3.8 %multiply_reduce_fusion = f32[64,2048]{1,0:T(8,128)S(1)} fusion(f32[64,6,2048]{2,1,0:T(8,128)} %reshape.155, f32[64,6]{1,0:T(8,128)S(1)} %copy.96), kind=kLoop, calls=%fused_computation.42 | loop fusion | flops 1441792 | bytes 3671552 | tf_op jit(solution)/shard_map/reduce_sum | solution.py:172
  360.7 0.8 fusion.37
  (37 shorter events, 0.3 us)
Async XLA Ops:
  6.5 126.4 %copy-start = (bf16[8,512,128]{2,1,0:T(8,128)(2,1)S(1)}, bf16[8,512,128]{2,1,0:T(8,128)(2,1)}, u32[]{:S(2)}) copy-start(bf16[8,512,128]{2,1,0:T(8,128)(2,1)} %param.21) | copy-start | bytes 3145732
  6.5 49.8 %all-gather.8.cloned.1.call-start = ((), (), s32[]{:S(2)}) async-start(), calls=%async_computation.3 | async-start | bytes 1392640 | tf_op jit(solution)/shard_map/all_gather | solution.py:65
  7.3 93.0 %all-gather.6.cloned.1.call-start = ((), (), s32[]{:S(2)}) async-start(), calls=%async_computation.2 | async-start | bytes 2785280 | tf_op jit(solution)/shard_map/all_gather | solution.py:66
  9.1 178.5 %all-gather.10.cloned.1.call-start = ((), (), s32[]{:S(2)}) async-start(), calls=%async_computation.4 | async-start | bytes 4325376 | tf_op jit(solution)/shard_map/all_gather | solution.py:124
  9.8 226.4 %all-gather.12.cloned.1.call-start = ((), (), s32[]{:S(2)}) async-start(), calls=%async_computation.5 | async-start | bytes 6127616 | tf_op jit(solution)/shard_map/all_gather | solution.py:151
  10.4 273.1 %all-gather.14.cloned.1.call-start = ((), (), s32[]{:S(2)}) async-start(), calls=%async_computation.6 | async-start | bytes 3063808 | tf_op jit(solution)/shard_map/all_gather | solution.py:152
  111.3 2.1 copy-start.1
  111.7 2.7 copy-start.4
  123.7 5.9 %copy-start.2 = (f32[64,8,2,1024]{3,1,2,0:T(8,128)S(1)}, f32[64,8,2,1024]{3,1,2,0:T(8,128)}, u32[]{:S(2)}) copy-start(f32[64,8,2,1024]{3,1,2,0:T(8,128)} %copy-done.1) | copy-start | bytes 12582916 | tf_op jit(solution)/shard_map/cond
  131.5 56.0 %copy-start.9 = (bf16[1,64,2048]{2,1,0:T(8,128)(2,1)S(1)}, bf16[1,64,2048]{2,1,0:T(8,128)(2,1)}, u32[]{:S(2)}) copy-start(bf16[1,64,2048]{2,1,0:T(8,128)(2,1)} %param.15) | copy-start | bytes 786436
  133.3 58.7 %copy-start.8 = (s32[512,64]{0,1:T(8,128)S(1)}, s32[512,64]{0,1:T(8,128)}, u32[]{:S(2)}) copy-start(s32[512,64]{0,1:T(8,128)} %convert_reduce_fusion) | copy-start | bytes 393220
  133.3 58.7 %copy-start.11 = (f32[2048]{0:T(1024)S(1)}, f32[2048]{0:T(1024)}, u32[]{:S(2)}) copy-start(f32[2048]{0:T(1024)} %param.23) | copy-start | bytes 24580
  191.2 0.8 copy-start.5
  194.1 53.4 %all-to-all-start = ((bf16[32,16,2048]{2,1,0:T(8,128)(2,1)}), bf16[32,16,2048]{2,1,0:T(8,128)(2,1)S(1)}, u32[]{:S(2)}, u32[]{:S(2)}) async-start(bf16[32,16,2048]{2,1,0:T(8,128)(2,1)} %bitcast.20), calls=%async_computation | async-start | bytes 4194304 | tf_op jit(solution)/shard_map/all_to_all | solution.py:149
  289.5 10.0 %copy-start.12 = (s32[1,64,6]{1,0,2:T(1,128)S(1)}, s32[1,64,6]{1,0,2:T(1,128)}, u32[]{:S(2)}) copy-start(s32[1,64,6]{1,0,2:T(1,128)} %param.25) | copy-start | bytes 4612
  289.5 10.3 %copy-start.10 = (bf16[2048,32]{0,1:T(8,128)(2,1)S(1)}, bf16[2048,32]{0,1:T(8,128)(2,1)}, u32[]{:S(2)}) copy-start(bf16[2048,32]{0,1:T(8,128)(2,1)} %param.24) | copy-start | bytes 393220
  289.5 60.4 %all-to-all-start.1 = ((bf16[32,16,2048]{2,1,0:T(8,128)(2,1)}), bf16[32,16,2048]{2,1,0:T(8,128)(2,1)S(1)}, u32[]{:S(2)}, u32[]{:S(2)}) async-start(bf16[32,16,2048]{2,1,0:T(8,128)(2,1)} %bitcast.102), calls=%async_computation.1 | async-start | bytes 4194304 | tf_op jit(solution)/shard_map/all_to_all | solution.py:163
  356.9 3.8 %copy-start.6 = (f32[64,2048]{1,0:T(8,128)S(1)}, f32[64,2048]{1,0:T(8,128)}, u32[]{:S(2)}) copy-start(f32[64,2048]{1,0:T(8,128)} %copy-done.5) | copy-start | bytes 1572868
Sparse Core Ops, SparseCore 0:
  9.5 46.7 all-gather.7
  58.4 41.7 all-gather.5
  103.4 84.0 all-gather.9
  189.5 46.6 all-gather.11
  238.1 45.3 all-gather.13
where the time goes:
time: 369 us; the launch traced here: 368 us
  waiting for transfers between devices  255 us (69%)
  local copies, waits for them, and re-layouts  34.7 us (9%)
  matrix products  33.2 us (9%)
  starting transfers between devices  17.3 us (5%)
  between operations  14 us (4%)
  other arithmetic  13.5 us (4%)
    all_gather x1, waiting for transfers between devices, local(): lax.all_gather(out_proj, 'expert', axis=1, tiled=True)  54.2 us
    all_to_all x1, waiting for transfers between devices, local(): lax.all_to_all(produced.reshape(-1, capacity, model_width), 'expert', spl...  48.6 us
    all_gather x1, waiting for transfers between devices, local(): prefix_piece = lax.all_gather(prefix_latent, 'seq', axis=1, tiled=True)  39 us
    all_gather x1, waiting for transfers between devices, local(): suffix_piece = lax.all_gather(suffix_latent, 'seq', axis=1, tiled=True)  36.3 us
    all_gather x1, waiting for transfers between devices, local(): lax.all_gather(expert_in, 'seq', axis=1, tiled=True)  34.9 us
    all_gather x1, waiting for transfers between devices, local(): lax.all_gather(expert_out, 'seq', axis=1, tiled=True)  28.3 us
    all_to_all x1, waiting for transfers between devices, local(): lax.all_to_all(outgoing, 'expert', split_axis=0, concat_axis=0, tiled=True)  11.3 us
    all_to_all x1, starting transfers between devices, local(): lax.all_to_all(produced.reshape(-1, capacity, model_width), 'expert', spl...  9.96 us
  transfers between devices with their start and end apart: 7, of which 7 were waited for; matrix products, arithmetic and copies ran while one was open for 17% of the time, Pallas kernels for 0%

commit v1 on v0

--- a/solution.py
+++ b/solution.py
@@ -63,7 +63,12 @@
         jnp.zeros((local_tokens, head_count, latent_width), jnp.float32),
     )
     suffix_piece = lax.all_gather(suffix_latent, "seq", axis=1, tiled=True)
-    prefix_piece = lax.all_gather(prefix_latent, "seq", axis=1, tiled=True)
+    ring = [prefix_latent]
+    for hop in range(15):
+        ring.append(lax.ppermute(ring[-1], "seq", [(dev, (dev + 1) % 16) for dev in range(16)]))
+    prefix_piece = jnp.roll(
+        jnp.concatenate(ring[::-1], axis=1), (lax.axis_index("seq") + 1) * ring[0].shape[1], axis=1
+    )
     piece_rows = suffix_piece.shape[1]
     suffix_keys = suffix_piece[0]
     key_positions = jnp.arange(piece_rows, dtype=jnp.int32)

time: 369 us -> 326 us (0.88)
  waiting for transfers between devices: 255 us -> 197 us
  local copies, waits for them, and re-layouts: 34.7 us -> 49.1 us
    ppermute x0 -> x15, waiting for transfers between devices: none -> 104 us  [local(): lax.ppermute(ring[-1], 'seq', [(dev, (dev + 1) % 16) for dev in range(16)])]
    all_gather x1, waiting for transfers between devices: 54.2 us -> 0.02 us  [local(): lax.all_gather(out_proj, 'expert', axis=1, tiled=True)]
    all_gather x1 -> x0, waiting for transfers between devices: 39 us -> none  [local(): prefix_piece = lax.all_gather(prefix_latent, 'seq', axis=1, tiled=True)]
    all_gather x1, waiting for transfers between devices: 36.3 us -> 0.02 us  [local(): suffix_piece = lax.all_gather(suffix_latent, 'seq', axis=1, tiled=True)]
    all_gather x1, waiting for transfers between devices: 34.9 us -> 2.2 us  [local(): lax.all_gather(expert_in, 'seq', axis=1, tiled=True)]
    all_gather x1, waiting for transfers between devices: 28.3 us -> 2.12 us  [local(): lax.all_gather(expert_out, 'seq', axis=1, tiled=True)]
    all_to_all x1, waiting for transfers between devices: 11.3 us -> 37.2 us  [local(): lax.all_to_all(outgoing, 'expert', split_axis=0, concat_axis=0, tiled=True)]
    concatenate x0 -> x1, local copies, waits for them, and re-layouts: none -> 13.1 us  [local(): jnp.roll(jnp.concatenate(ring[::-1], axis=1), (lax.axis_index('seq') + 1)...]
  transfers between devices with their start and end apart: 7 -> 21, of which waited for: 7 -> 19; matrix products, arithmetic and copies ran while one was open for 17% -> 22% of each run, Pallas kernels for 0% -> 0%
where the time goes in v1:
time: 326 us; the launch traced here: 324 us
  waiting for transfers between devices  197 us (60%)
  local copies, waits for them, and re-layouts  49.1 us (15%)
  matrix products  33.5 us (10%)
  starting transfers between devices  17.3 us (5%)
  between operations  14.1 us (4%)
  other arithmetic  13.6 us (4%)
    ppermute x15, waiting for transfers between devices, local(): lax.ppermute(ring[-1], 'seq', [(dev, (dev + 1) % 16) for dev in range(16)])  104 us
    all_to_all x1, waiting for transfers between devices, local(): lax.all_to_all(produced.reshape(-1, capacity, model_width), 'expert', spl...  48.6 us
    all_to_all x1, waiting for transfers between devices, local(): lax.all_to_all(outgoing, 'expert', split_axis=0, concat_axis=0, tiled=True)  37.2 us
    concatenate x1, local copies, waits for them, and re-layouts, local(): jnp.roll(jnp.concatenate(ring[::-1], axis=1), (lax.axis_index('seq') + 1)...  13.1 us
    all_to_all x1, starting transfers between devices, local(): lax.all_to_all(produced.reshape(-1, capacity, model_width), 'expert', spl...  9.96 us
    dot_general x1, matrix products, local(): gate_up = jnp.dot(all_rows, full_in[0], preferred_element_type=jnp.float32)  7.75 us
    unnamed x45, local copies, waits for them, and re-layouts  7.17 us
    all_to_all x1, starting transfers between devices, local(): lax.all_to_all(outgoing, 'expert', split_axis=0, concat_axis=0, tiled=True)  7.16 us
  transfers between devices with their start and end apart: 21, of which 19 were waited for; matrix products, arithmetic and copies ran while one was open for 22% of the time, Pallas kernels for 0%

profile of v1, /device:TPU:16, one launch (start us, length us, event | category | flops | bytes accessed | tf_op | source)
XLA Modules:
  0.0 324.2 jit_solution(1581888031089553037)
XLA Ops:
  6.5 0.7 all-gather.5.cloned.1.call-update
  7.3 0.7 all-gather.7.cloned.1.call-update
  8.1 0.7 all-gather.9.cloned.1.call-update
  8.8 1.1 copy.90
  9.9 12.9 %collective-permute-done = bf16[2,64,576]{1,2,0:T(8,128)(2,1)S(1)} collective-permute-done((bf16[2,64,576]{1,2,0:T(8,128)(2,1)S(1)}, bf16[2,64,576]{1,2,0:T(8,128)(2,1)S(1)}, u32[]{:S(2)}, u32[]{:S(2)}) %collective-permute-start) | collective-permute-done | bytes 147488 | tf_op jit(solution)/shard_map/ppermute | solution.py:68
  22.8 0.7 copy-done.6
  23.5 7.4 %collective-permute-done.1 = bf16[2,64,576]{1,2,0:T(8,128)(2,1)S(1)} collective-permute-done((bf16[2,64,576]{1,2,0:T(8,128)(2,1)S(1)}, bf16[2,64,576]{1,2,0:T(8,128)(2,1)S(1)}, u32[]{:S(2)}, u32[]{:S(2)}) %collective-permute-start.1) | collective-permute-done | bytes 147488 | tf_op jit(solution)/shard_map/ppermute | solution.py:68
  30.9 0.7 copy-done.7
  31.6 8.3 %collective-permute-done.2 = bf16[2,64,576]{1,2,0:T(8,128)(2,1)S(1)} collective-permute-done((bf16[2,64,576]{1,2,0:T(8,128)(2,1)S(1)}, bf16[2,64,576]{1,2,0:T(8,128)(2,1)S(1)}, u32[]{:S(2)}, u32[]{:S(2)}) %collective-permute-start.2) | collective-permute-done | bytes 147488 | tf_op jit(solution)/shard_map/ppermute | solution.py:68
  40.0 0.7 copy-done.8
  40.7 8.2 %collective-permute-done.3 = bf16[2,64,576]{1,2,0:T(8,128)(2,1)S(1)} collective-permute-done((bf16[2,64,576]{1,2,0:T(8,128)(2,1)S(1)}, bf16[2,64,576]{1,2,0:T(8,128)(2,1)S(1)}, u32[]{:S(2)}, u32[]{:S(2)}) %collective-permute-start.3) | collective-permute-done | bytes 147488 | tf_op jit(solution)/shard_map/ppermute | solution.py:68
  48.9 0.7 copy-done.9
  49.7 7.6 %collective-permute-done.4 = bf16[2,64,576]{1,2,0:T(8,128)(2,1)S(1)} collective-permute-done((bf16[2,64,576]{1,2,0:T(8,128)(2,1)S(1)}, bf16[2,64,576]{1,2,0:T(8,128)(2,1)S(1)}, u32[]{:S(2)}, u32[]{:S(2)}) %collective-permute-start.4) | collective-permute-done | bytes 147488 | tf_op jit(solution)/shard_map/ppermute | solution.py:68
  57.2 0.7 copy-done.10
  58.0 7.4 %collective-permute-done.5 = bf16[2,64,576]{1,2,0:T(8,128)(2,1)S(1)} collective-permute-done((bf16[2,64,576]{1,2,0:T(8,128)(2,1)S(1)}, bf16[2,64,576]{1,2,0:T(8,128)(2,1)S(1)}, u32[]{:S(2)}, u32[]{:S(2)}) %collective-permute-start.5) | collective-permute-done | bytes 147488 | tf_op jit(solution)/shard_map/ppermute | solution.py:68
  65.3 0.7 copy-done.11
  66.0 7.4 %collective-permute-done.6 = bf16[2,64,576]{1,2,0:T(8,128)(2,1)S(1)} collective-permute-done((bf16[2,64,576]{1,2,0:T(8,128)(2,1)S(1)}, bf16[2,64,576]{1,2,0:T(8,128)(2,1)S(1)}, u32[]{:S(2)}, u32[]{:S(2)}) %collective-permute-start.6) | collective-permute-done | bytes 147488 | tf_op jit(solution)/shard_map/ppermute | solution.py:68
  73.4 0.8 copy.101
  74.4 6.4 %collective-permute-done.7 = bf16[2,64,576]{1,2,0:T(8,128)(2,1)S(1)} collective-permute-done((bf16[2,64,576]{1,2,0:T(8,128)(2,1)S(1)}, bf16[2,64,576]{1,2,0:T(8,128)(2,1)S(1)}, u32[]{:S(2)}, u32[]{:S(2)}) %collective-permute-start.7) | collective-permute-done | bytes 147488 | tf_op jit(solution)/shard_map/ppermute | solution.py:68
  80.8 0.9 reduce-window.19
  81.7 6.5 %collective-permute-done.8 = bf16[2,64,576]{1,2,0:T(8,128)(2,1)S(1)} collective-permute-done((bf16[2,64,576]{1,2,0:T(8,128)(2,1)S(1)}, bf16[2,64,576]{1,2,0:T(8,128)(2,1)S(1)}, u32[]{:S(2)}, u32[]{:S(2)}) %collective-permute-start.8) | collective-permute-done | bytes 147488 | tf_op jit(solution)/shard_map/ppermute | solution.py:68
  88.8 6.7 %collective-permute-done.9 = bf16[2,64,576]{1,2,0:T(8,128)(2,1)S(1)} collective-permute-done((bf16[2,64,576]{1,2,0:T(8,128)(2,1)S(1)}, bf16[2,64,576]{1,2,0:T(8,128)(2,1)S(1)}, u32[]{:S(2)}, u32[]{:S(2)}) %collective-permute-start.9) | collective-permute-done | bytes 147488 | tf_op jit(solution)/shard_map/ppermute | solution.py:68
  95.5 0.9 reduce-window.18
  96.5 6.4 %collective-permute-done.10 = bf16[2,64,576]{1,2,0:T(8,128)(2,1)S(1)} collective-permute-done((bf16[2,64,576]{1,2,0:T(8,128)(2,1)S(1)}, bf16[2,64,576]{1,2,0:T(8,128)(2,1)S(1)}, u32[]{:S(2)}, u32[]{:S(2)}) %collective-permute-start.10) | collective-permute-done | bytes 147488 | tf_op jit(solution)/shard_map/ppermute | solution.py:68
  102.9 7.3 %collective-permute-done.11 = bf16[2,64,576]{1,2,0:T(8,128)(2,1)S(1)} collective-permute-done((bf16[2,64,576]{1,2,0:T(8,128)(2,1)S(1)}, bf16[2,64,576]{1,2,0:T(8,128)(2,1)S(1)}, u32[]{:S(2)}, u32[]{:S(2)}) %collective-permute-start.11) | collective-permute-done | bytes 147488 | tf_op jit(solution)/shard_map/ppermute | solution.py:68
  110.3 0.7 select_reduce_fusion.3
  111.1 6.5 %collective-permute-done.12 = bf16[2,64,576]{1,2,0:T(8,128)(2,1)S(1)} collective-permute-done((bf16[2,64,576]{1,2,0:T(8,128)(2,1)S(1)}, bf16[2,64,576]{1,2,0:T(8,128)(2,1)S(1)}, u32[]{:S(2)}, u32[]{:S(2)}) %collective-permute-start.12) | collective-permute-done | bytes 147488 | tf_op jit(solution)/shard_map/ppermute | solution.py:68
  117.6 0.7 compare_reduce_fusion
  118.2 2.4 reshape_squeeze.3
  121.4 0.8 convert_reduce_fusion
  122.2 2.8 collective-permute-done.13
  125.1 2.5 convolution_multiply_fusion
  127.7 2.4 copy.93
  130.1 2.6 collective-permute-done.14
  132.7 13.1 %concatenate.24 = bf16[2,2048,576]{1,2,0:T(8,128)(2,1)} concatenate(bf16[2,64,576]{1,2,0:T(8,128)(2,1)} %collective-permute-done.14, bf16[2,64,576]{1,2,0:T(8,128)(2,1)} %collective-permute-done.13, bf16[2,64,576]{1,2,0:T(8,128)(2,1)} %copy-done.18, bf16[2,64,576]{1,2,0:T(8,128)(2,1)} %copy-done.17, bf16[2,64,576]{1,2,0:T(8,128)(2,1)} %copy-done.16, ...), dimensions={1} | concatenate | bytes 9437184 | tf_op jit(solution)/shard_map/jit(_roll_dynamic)/concatenate | solution.py:69
  145.8 4.3 %constant_dynamic-slice_fusion = bf16[2,1024,576]{1,2,0:T(8,128)(2,1)} fusion(bf16[2,2048,576]{1,2,0:T(8,128)(2,1)} %concatenate.24, s32[]{:T(128)S(6)} %select_n.51), kind=kLoop, calls=%fused_computation.94 | loop fusion | bytes 4718596 | tf_op jit(solution)/shard_map/jit(_roll_dynamic)/dynamic_slice | solution.py:69
  150.1 24.5 %conditional.1 = (f32[64,8,512]{2,1,0:T(8,128)}, f32[64,8]{1,0:T(8,128)S(1)}) conditional(s32[]{:T(128)} %convert_element_type.64, (s32[64]{0:T(128)S(1)}, s32[64,2]{1,0:T(8,128)S(1)}, pred[64,1024]{1,0:T(8,128)(4,1)S(1)}, bf16[64,8,576]{2,1,0:T(8,128)(2,1)}, bf16[2,1024,576]{1,2,0:T(8,128)(2,1)}, /*index=5*/f32[64,8,1024]{2,1,0:T(8,128)S(1)}, ...), branch_computations={%region_5.8_spmd, %region_8.11_spmd} | conditional | flops 2843409920 | bytes 78001224 | solution.py:121
  150.1 3.7 %fusion.10 = f32[64,8,2,1024]{3,1,2,0:T(8,128)S(1)} fusion(bf16[2,1024,576]{1,2,0:T(8,128)(2,1)} %get-tuple-element.38, bf16[64,8,576]{2,1,0:T(8,128)(2,1)} %get-tuple-element.37), kind=kOutput, calls=%fused_computation.14 | convolution fusion | flops 1209008128 | bytes 7143424 | tf_op jit(solution)/shard_map/cond/branch_0_fun/thk,pnk->thpn/dot_general | solution.py:100
  154.2 1.2 select_reduce_fusion
  155.4 0.4 copy-done.1
  155.9 3.1 slice.20
  159.0 4.0 %copy.86 = bf16[2,1024,512]{2,1,0:T(8,128)(2,1)} copy(bf16[2,1024,512]{1,2,0:T(8,128)(2,1)} %slice.20) | data formatting | bytes 4194304 | tf_op jit(solution)/shard_map/cond/branch_0_fun/slice | solution.py:115
  163.0 2.4 copy.94
  165.4 1.3 slice.35
  166.7 6.0 %fusion.2 = f32[64,8,512]{2,1,0:T(8,128)} fusion(bf16[2048,512]{1,0:T(8,128)(2,1)} %bitcast.104, bf16[1024,512]{1,0:T(8,128)(2,1)S(1)} %slice.35, f32[64,8,2048]{2,1,0:T(8,128)} %bitcast.98, f32[64,8,1024]{2,1,0:T(8,128)S(1)} %get-tuple-element.36, f32[64,8]{1,0:T(8,128)S(1)} %broadcast_maximum_fusion, pred[64,3072]{1,0:T(8,128)(4,1)S(1)} %pad_add_fusion), kind=kOutput, calls=%fused_computation.7 | convolution fusion | flops 1623195648 | bytes 10684416 | tf_op jit(solution)/shard_map/cond/branch_0_fun/thn,nl->thl/dot_general | solution.py:19
  172.7 1.8 fusion.1
  174.6 1.5 divide_convert_fusion
  176.1 0.4 fusion.33
  176.5 3.8 %multiply_reduce_fusion.1 = (f32[64]{0:T(128)S(1)}, f32[64,2048]{1,0:T(8,128)S(1)}) fusion(bf16[1024,2048]{0,1:T(8,128)(2,1)} %all-gather.7.cloned.1.call-done, bf16[8,8,8,128]{3,2,1,0:T(8,128)(2,1)S(1)} %fusion.33, bf16[1,64,2048]{2,1,0:T(8,128)(2,1)S(1)} %copy-done.20), kind=kOutput, calls=%fused_computation.60 | convolution fusion | flops 268959680 | bytes 5112064 | tf_op jit(solution)/shard_map/dot_general | solution.py:127
  180.3 0.8 copy-done.4
  181.2 2.1 convolution_convert_fusion.1
  183.3 7.2 %all-to-all-start = ((bf16[32,16,2048]{2,1,0:T(8,128)(2,1)}), bf16[32,16,2048]{2,1,0:T(8,128)(2,1)S(1)}, u32[]{:S(2)}, u32[]{:S(2)}) async-start(bf16[32,16,2048]{2,1,0:T(8,128)(2,1)} %bitcast.20), calls=%async_computation | async-start | bytes 4194304 | tf_op jit(solution)/shard_map/all_to_all | solution.py:154
  190.4 2.2 all-gather.9.cloned.1.call-done
  192.6 37.2 %all-to-all-done = bf16[32,16,2048]{2,1,0:T(8,128)(2,1)S(1)} async-done(((bf16[32,16,2048]{2,1,0:T(8,128)(2,1)}), bf16[32,16,2048]{2,1,0:T(8,128)(2,1)S(1)}, u32[]{:S(2)}, u32[]{:S(2)}) %all-to-all-start) | async-done | bytes 2097184 | tf_op jit(solution)/shard_map/all_to_all | solution.py:154
  229.9 7.8 %fusion.28 = f32[512,1408]{1,0:T(8,128)} fusion(bf16[512,2048]{1,0:T(8,128)(2,1)S(1)} %bitcast.103, bf16[1,2048,1408]{2,1,0:T(8,128)(2,1)} %all-gather.9.cloned.1.call-done), kind=kOutput, calls=%fused_computation.40 | convolution fusion | flops 2952790016 | bytes 10747904 | tf_op jit(solution)/shard_map/dot_general | solution.py:160
  237.6 2.1 all-gather.11.cloned.1.call-done
  239.7 6.0 %convolution_convert_fusion = bf16[512,2048]{1,0:T(8,128)(2,1)} fusion(bf16[1,2048,704]{1,2,0:T(8,128)(2,1)} %all-gather.11.cloned.1.call-done, f32[512,1408]{1,0:T(8,128)} %fusion.28), kind=kOutput, calls=%fused_computation.43 | convolution fusion | flops 1479606272 | bytes 8126464 | tf_op jit(solution)/shard_map/dot_general | solution.py:165
  245.7 10.0 %all-to-all-start.1 = ((bf16[32,16,2048]{2,1,0:T(8,128)(2,1)}), bf16[32,16,2048]{2,1,0:T(8,128)(2,1)S(1)}, u32[]{:S(2)}, u32[]{:S(2)}) async-start(bf16[32,16,2048]{2,1,0:T(8,128)(2,1)} %bitcast.102), calls=%async_computation.1 | async-start | bytes 4194304 | tf_op jit(solution)/shard_map/all_to_all | solution.py:168
  256.0 1.3 fusion.50
  257.5 48.6 %all-to-all-done.1 = bf16[32,16,2048]{2,1,0:T(8,128)(2,1)S(1)} async-done(((bf16[32,16,2048]{2,1,0:T(8,128)(2,1)}), bf16[32,16,2048]{2,1,0:T(8,128)(2,1)S(1)}, u32[]{:S(2)}, u32[]{:S(2)}) %all-to-all-start.1) | async-done | bytes 2097184 | tf_op jit(solution)/shard_map/all_to_all | solution.py:168
  306.1 3.1 gather_fusion
  309.2 3.9 %reshape.155 = f32[64,6,2048]{2,1,0:T(8,128)} reshape(bf16[384,2048]{1,0:T(8,128)(2,1)} %gather_fusion) | data formatting | bytes 4718592 | tf_op jit(solution)/shard_map/convert_element_type | solution.py:177
  313.1 3.8 %multiply_reduce_fusion = f32[64,2048]{1,0:T(8,128)S(1)} fusion(f32[64,6,2048]{2,1,0:T(8,128)} %reshape.155, f32[64,6]{1,0:T(8,128)S(1)} %copy.100), kind=kLoop, calls=%fused_computation.42 | loop fusion | flops 1441792 | bytes 3671552 | tf_op jit(solution)/shard_map/reduce_sum | solution.py:177
  316.9 0.8 fusion.37
  (89 shorter events, 2.3 us)
Async XLA Ops:
  6.5 169.6 %copy-start = (bf16[8,512,128]{2,1,0:T(8,128)(2,1)S(1)}, bf16[8,512,128]{2,1,0:T(8,128)(2,1)}, u32[]{:S(2)}) copy-start(bf16[8,512,128]{2,1,0:T(8,128)(2,1)} %param.21) | copy-start | bytes 3145732
  6.5 118.6 %all-gather.5.cloned.1.call-start = ((), (), s32[]{:S(2)}) async-start(), calls=%async_computation.2 | async-start | bytes 1392640 | tf_op jit(solution)/shard_map/all_gather | solution.py:65
  7.3 169.3 %all-gather.7.cloned.1.call-start = ((), (), s32[]{:S(2)}) async-start(), calls=%async_computation.3 | async-start | bytes 4325376 | tf_op jit(solution)/shard_map/all_gather | solution.py:129
  8.0 184.6 %all-gather.9.cloned.1.call-start = ((), (), s32[]{:S(2)}) async-start(), calls=%async_computation.4 | async-start | bytes 6127616 | tf_op jit(solution)/shard_map/all_gather | solution.py:156
  8.7 231.0 %all-gather.11.cloned.1.call-start = ((), (), s32[]{:S(2)}) async-start(), calls=%async_computation.5 | async-start | bytes 3063808 | tf_op jit(solution)/shard_map/all_gather | solution.py:157
  9.9 12.9 %collective-permute-start = (bf16[2,64,576]{1,2,0:T(8,128)(2,1)S(1)}, bf16[2,64,576]{1,2,0:T(8,128)(2,1)S(1)}, u32[]{:S(2)}, u32[]{:S(2)}) collective-permute-start(bf16[2,64,576]{1,2,0:T(8,128)(2,1)S(1)} %copy.90), channel_id=1, source_target_pairs={{0,32},{32,64},{64,96},{96,128},{128,160},{160,192},{192,224},{224... | collective-permute-start | bytes 442376 | tf_op jit(solution)/shard_map/ppermute | solution.py:68
  22.8 0.7 copy-start.6
  23.5 7.4 %collective-permute-start.1 = (bf16[2,64,576]{1,2,0:T(8,128)(2,1)S(1)}, bf16[2,64,576]{1,2,0:T(8,128)(2,1)S(1)}, u32[]{:S(2)}, u32[]{:S(2)}) collective-permute-start(bf16[2,64,576]{1,2,0:T(8,128)(2,1)S(1)} %collective-permute-done), channel_id=1, source_target_pairs={{0,32},{32,64},{64,96},{96,128},{128,160},{160,192},{192,224},{224... | collective-permute-start | bytes 442376 | tf_op jit(solution)/shard_map/ppermute | solution.py:68
  30.9 0.7 copy-start.7
  31.6 8.3 %collective-permute-start.2 = (bf16[2,64,576]{1,2,0:T(8,128)(2,1)S(1)}, bf16[2,64,576]{1,2,0:T(8,128)(2,1)S(1)}, u32[]{:S(2)}, u32[]{:S(2)}) collective-permute-start(bf16[2,64,576]{1,2,0:T(8,128)(2,1)S(1)} %collective-permute-done.1), channel_id=1, source_target_pairs={{0,32},{32,64},{64,96},{96,128},{128,160},{160,192},{192,224},{224... | collective-permute-start | bytes 442376 | tf_op jit(solution)/shard_map/ppermute | solution.py:68
  40.0 0.7 copy-start.8
  40.7 8.2 %collective-permute-start.3 = (bf16[2,64,576]{1,2,0:T(8,128)(2,1)S(1)}, bf16[2,64,576]{1,2,0:T(8,128)(2,1)S(1)}, u32[]{:S(2)}, u32[]{:S(2)}) collective-permute-start(bf16[2,64,576]{1,2,0:T(8,128)(2,1)S(1)} %collective-permute-done.2), channel_id=1, source_target_pairs={{0,32},{32,64},{64,96},{96,128},{128,160},{160,192},{192,224},{224... | collective-permute-start | bytes 442376 | tf_op jit(solution)/shard_map/ppermute | solution.py:68
  48.9 0.7 copy-start.9
  49.6 7.6 %collective-permute-start.4 = (bf16[2,64,576]{1,2,0:T(8,128)(2,1)S(1)}, bf16[2,64,576]{1,2,0:T(8,128)(2,1)S(1)}, u32[]{:S(2)}, u32[]{:S(2)}) collective-permute-start(bf16[2,64,576]{1,2,0:T(8,128)(2,1)S(1)} %collective-permute-done.3), channel_id=1, source_target_pairs={{0,32},{32,64},{64,96},{96,128},{128,160},{160,192},{192,224},{224... | collective-permute-start | bytes 442376 | tf_op jit(solution)/shard_map/ppermute | solution.py:68
  57.2 0.7 copy-start.10
  58.0 7.4 %collective-permute-start.5 = (bf16[2,64,576]{1,2,0:T(8,128)(2,1)S(1)}, bf16[2,64,576]{1,2,0:T(8,128)(2,1)S(1)}, u32[]{:S(2)}, u32[]{:S(2)}) collective-permute-start(bf16[2,64,576]{1,2,0:T(8,128)(2,1)S(1)} %collective-permute-done.4), channel_id=1, source_target_pairs={{0,32},{32,64},{64,96},{96,128},{128,160},{160,192},{192,224},{224... | collective-permute-start | bytes 442376 | tf_op jit(solution)/shard_map/ppermute | solution.py:68
  65.3 0.7 copy-start.11
  66.0 7.4 %collective-permute-start.6 = (bf16[2,64,576]{1,2,0:T(8,128)(2,1)S(1)}, bf16[2,64,576]{1,2,0:T(8,128)(2,1)S(1)}, u32[]{:S(2)}, u32[]{:S(2)}) collective-permute-start(bf16[2,64,576]{1,2,0:T(8,128)(2,1)S(1)} %collective-permute-done.5), channel_id=1, source_target_pairs={{0,32},{32,64},{64,96},{96,128},{128,160},{160,192},{192,224},{224... | collective-permute-start | bytes 442376 | tf_op jit(solution)/shard_map/ppermute | solution.py:68
  73.4 51.6 %copy-start.12 = (bf16[2,64,576]{1,2,0:T(8,128)(2,1)}, bf16[2,64,576]{1,2,0:T(8,128)(2,1)S(1)}, u32[]{:S(2)}) copy-start(bf16[2,64,576]{1,2,0:T(8,128)(2,1)S(1)} %collective-permute-done.6) | copy-start | bytes 442372
  73.4 7.4 %collective-permute-start.7 = (bf16[2,64,576]{1,2,0:T(8,128)(2,1)S(1)}, bf16[2,64,576]{1,2,0:T(8,128)(2,1)S(1)}, u32[]{:S(2)}, u32[]{:S(2)}) collective-permute-start(bf16[2,64,576]{1,2,0:T(8,128)(2,1)S(1)} %collective-permute-done.6), channel_id=1, source_target_pairs={{0,32},{32,64},{64,96},{96,128},{128,160},{160,192},{192,224},{224... | collective-permute-start | bytes 442376 | tf_op jit(solution)/shard_map/ppermute | solution.py:68
  80.8 44.3 %copy-start.13 = (bf16[2,64,576]{1,2,0:T(8,128)(2,1)}, bf16[2,64,576]{1,2,0:T(8,128)(2,1)S(1)}, u32[]{:S(2)}) copy-start(bf16[2,64,576]{1,2,0:T(8,128)(2,1)S(1)} %collective-permute-done.7) | copy-start | bytes 442372
  80.8 7.4 %collective-permute-start.8 = (bf16[2,64,576]{1,2,0:T(8,128)(2,1)S(1)}, bf16[2,64,576]{1,2,0:T(8,128)(2,1)S(1)}, u32[]{:S(2)}, u32[]{:S(2)}) collective-permute-start(bf16[2,64,576]{1,2,0:T(8,128)(2,1)S(1)} %collective-permute-done.7), channel_id=1, source_target_pairs={{0,32},{32,64},{64,96},{96,128},{128,160},{160,192},{192,224},{224... | collective-permute-start | bytes 442376 | tf_op jit(solution)/shard_map/ppermute | solution.py:68
  88.1 36.9 %copy-start.14 = (bf16[2,64,576]{1,2,0:T(8,128)(2,1)}, bf16[2,64,576]{1,2,0:T(8,128)(2,1)S(1)}, u32[]{:S(2)}) copy-start(bf16[2,64,576]{1,2,0:T(8,128)(2,1)S(1)} %collective-permute-done.8) | copy-start | bytes 442372
  88.1 7.4 %collective-permute-start.9 = (bf16[2,64,576]{1,2,0:T(8,128)(2,1)S(1)}, bf16[2,64,576]{1,2,0:T(8,128)(2,1)S(1)}, u32[]{:S(2)}, u32[]{:S(2)}) collective-permute-start(bf16[2,64,576]{1,2,0:T(8,128)(2,1)S(1)} %collective-permute-done.8), channel_id=1, source_target_pairs={{0,32},{32,64},{64,96},{96,128},{128,160},{160,192},{192,224},{224... | collective-permute-start | bytes 442376 | tf_op jit(solution)/shard_map/ppermute | solution.py:68
  95.5 29.6 %copy-start.15 = (bf16[2,64,576]{1,2,0:T(8,128)(2,1)}, bf16[2,64,576]{1,2,0:T(8,128)(2,1)S(1)}, u32[]{:S(2)}) copy-start(bf16[2,64,576]{1,2,0:T(8,128)(2,1)S(1)} %collective-permute-done.9) | copy-start | bytes 442372
  95.5 7.4 %collective-permute-start.10 = (bf16[2,64,576]{1,2,0:T(8,128)(2,1)S(1)}, bf16[2,64,576]{1,2,0:T(8,128)(2,1)S(1)}, u32[]{:S(2)}, u32[]{:S(2)}) collective-permute-start(bf16[2,64,576]{1,2,0:T(8,128)(2,1)S(1)} %collective-permute-done.9), channel_id=1, source_target_pairs={{0,32},{32,64},{64,96},{96,128},{128,160},{160,192},{192,224},{224... | collective-permute-start | bytes 442376 | tf_op jit(solution)/shard_map/ppermute | solution.py:68
  102.8 22.2 %copy-start.16 = (bf16[2,64,576]{1,2,0:T(8,128)(2,1)}, bf16[2,64,576]{1,2,0:T(8,128)(2,1)S(1)}, u32[]{:S(2)}) copy-start(bf16[2,64,576]{1,2,0:T(8,128)(2,1)S(1)} %collective-permute-done.10) | copy-start | bytes 442372
  102.8 7.4 %collective-permute-start.11 = (bf16[2,64,576]{1,2,0:T(8,128)(2,1)S(1)}, bf16[2,64,576]{1,2,0:T(8,128)(2,1)S(1)}, u32[]{:S(2)}, u32[]{:S(2)}) collective-permute-start(bf16[2,64,576]{1,2,0:T(8,128)(2,1)S(1)} %collective-permute-done.10), channel_id=1, source_target_pairs={{0,32},{32,64},{64,96},{96,128},{128,160},{160,192},{192,224},{224... | collective-permute-start | bytes 442376 | tf_op jit(solution)/shard_map/ppermute | solution.py:68
  110.2 14.9 %copy-start.17 = (bf16[2,64,576]{1,2,0:T(8,128)(2,1)}, bf16[2,64,576]{1,2,0:T(8,128)(2,1)S(1)}, u32[]{:S(2)}) copy-start(bf16[2,64,576]{1,2,0:T(8,128)(2,1)S(1)} %collective-permute-done.11) | copy-start | bytes 442372
  110.2 7.4 %collective-permute-start.12 = (bf16[2,64,576]{1,2,0:T(8,128)(2,1)S(1)}, bf16[2,64,576]{1,2,0:T(8,128)(2,1)S(1)}, u32[]{:S(2)}, u32[]{:S(2)}) collective-permute-start(bf16[2,64,576]{1,2,0:T(8,128)(2,1)S(1)} %collective-permute-done.11), channel_id=1, source_target_pairs={{0,32},{32,64},{64,96},{96,128},{128,160},{160,192},{192,224},{224... | collective-permute-start | bytes 442376 | tf_op jit(solution)/shard_map/ppermute | solution.py:68
  117.6 7.5 %copy-start.18 = (bf16[2,64,576]{1,2,0:T(8,128)(2,1)}, bf16[2,64,576]{1,2,0:T(8,128)(2,1)S(1)}, u32[]{:S(2)}) copy-start(bf16[2,64,576]{1,2,0:T(8,128)(2,1)S(1)} %collective-permute-done.12) | copy-start | bytes 442372
  117.6 7.5 %collective-permute-start.13 = (bf16[2,64,576]{1,2,0:T(8,128)(2,1)S(1)}, bf16[2,64,576]{1,2,0:T(8,128)(2,1)}, u32[]{:S(2)}, u32[]{:S(2)}) collective-permute-start(bf16[2,64,576]{1,2,0:T(8,128)(2,1)S(1)} %collective-permute-done.12), channel_id=1, source_target_pairs={{0,32},{32,64},{64,96},{96,128},{128,160},{160,192},{192,224},{224... | collective-permute-start | bytes 442376 | tf_op jit(solution)/shard_map/ppermute | solution.py:68
  125.0 7.7 %collective-permute-start.14 = (bf16[2,64,576]{1,2,0:T(8,128)(2,1)}, bf16[2,64,576]{1,2,0:T(8,128)(2,1)}, u32[]{:S(2)}, u32[]{:S(2)}) collective-permute-start(bf16[2,64,576]{1,2,0:T(8,128)(2,1)} %collective-permute-done.13), channel_id=1, source_target_pairs={{0,32},{32,64},{64,96},{96,128},{128,160},{160,192},{192,224},{224... | collective-permute-start | bytes 442376 | tf_op jit(solution)/shard_map/ppermute | solution.py:68
  153.8 2.0 copy-start.1
  166.7 6.0 %copy-start.2 = (f32[64,8,2,1024]{3,1,2,0:T(8,128)S(1)}, f32[64,8,2,1024]{3,1,2,0:T(8,128)}, u32[]{:S(2)}) copy-start(f32[64,8,2,1024]{3,1,2,0:T(8,128)} %copy-done.1) | copy-start | bytes 12582916 | tf_op jit(solution)/shard_map/cond
  174.6 1.9 copy-start.20
  176.5 4.7 %copy-start.19 = (s32[512,64]{0,1:T(8,128)S(1)}, s32[512,64]{0,1:T(8,128)}, u32[]{:S(2)}) copy-start(s32[512,64]{0,1:T(8,128)} %convert_reduce_fusion) | copy-start | bytes 393220
  176.5 4.7 %copy-start.22 = (f32[2048]{0:T(1024)S(1)}, f32[2048]{0:T(1024)}, u32[]{:S(2)}) copy-start(f32[2048]{0:T(1024)} %param.23) | copy-start | bytes 24580
  180.3 0.9 copy-start.4
  183.3 46.6 %all-to-all-start = ((bf16[32,16,2048]{2,1,0:T(8,128)(2,1)}), bf16[32,16,2048]{2,1,0:T(8,128)(2,1)S(1)}, u32[]{:S(2)}, u32[]{:S(2)}) async-start(bf16[32,16,2048]{2,1,0:T(8,128)(2,1)} %bitcast.20), calls=%async_computation | async-start | bytes 4194304 | tf_op jit(solution)/shard_map/all_to_all | solution.py:154
  245.7 10.0 %copy-start.23 = (s32[1,64,6]{1,0,2:T(1,128)S(1)}, s32[1,64,6]{1,0,2:T(1,128)}, u32[]{:S(2)}) copy-start(s32[1,64,6]{1,0,2:T(1,128)} %param.25) | copy-start | bytes 4612
  245.7 10.3 %copy-start.21 = (bf16[2048,32]{0,1:T(8,128)(2,1)S(1)}, bf16[2048,32]{0,1:T(8,128)(2,1)}, u32[]{:S(2)}) copy-start(bf16[2048,32]{0,1:T(8,128)(2,1)} %param.24) | copy-start | bytes 393220
  245.7 60.4 %all-to-all-start.1 = ((bf16[32,16,2048]{2,1,0:T(8,128)(2,1)}), bf16[32,16,2048]{2,1,0:T(8,128)(2,1)S(1)}, u32[]{:S(2)}, u32[]{:S(2)}) async-start(bf16[32,16,2048]{2,1,0:T(8,128)(2,1)} %bitcast.102), calls=%async_computation.1 | async-start | bytes 4194304 | tf_op jit(solution)/shard_map/all_to_all | solution.py:168
  313.1 3.8 %copy-start.5 = (f32[64,2048]{1,0:T(8,128)S(1)}, f32[64,2048]{1,0:T(8,128)}, u32[]{:S(2)}) copy-start(f32[64,2048]{1,0:T(8,128)} %copy-done.4) | copy-start | bytes 1572868
Sparse Core Ops, SparseCore 0:
  9.5 46.7 all-gather.4
  59.5 84.4 all-gather.6
  146.1 46.5 all-gather.8
  194.5 45.1 all-gather.10
